TPU v7x, 128 devices: a whole 4x4x4 slice. The times are simulated.
128 devices in a mesh: ctx: 16 (over z, y), head: 8 (over x, core).
Axes of the slice: x: 4, y: 4, z: 4, core: 2. Of those that a mesh axis runs over, the one named last changes fastest.
Arguments:
- queries: bfloat16 [32768, 8192], P(('ctx', 'head')), may hold values from -150 to 150
- key_states: bfloat16 [32768, 1024], P(('ctx', 'head')), may hold values from -10 to 10
- value_states: bfloat16 [32768, 1024], P(('ctx', 'head')), may hold values from -6 to 6
- page_ids: int32 [256], replicated, may hold values from 0 to 63, never falling along the last dimension, each value on 1 to 8 neighbouring positions
- ref_group: int32 [256, 4], replicated, may hold values from 0 to 15, all different within a row; in each aligned block of 16 rows (0 to 15, 16 to 31, ...) at most 4 rows name the same one
- ref_slot: int32 [256, 4], replicated, may hold values from 0 to 15
Outputs:
- attended: bfloat16 [32768, 8192], P(('ctx', 'head'))
Inputs may be any that keep to these rules, and one draw needn't show every extreme that they name: `page_ids`: ids never fall; every page has 1 to 8 blocks and one has exactly 8. `ref_group`: a row's 4 values differ; the rows of the 16 blocks of one ctx group name every ctx group exactly 4 times.
All inputs are finite; a program needn't handle non-finite values.
Results may differ from a plain program's by a relative error of at most 0.0042.
Values may be sent and summed in bfloat16 or wider, within the bound.
No kernel may reach another device: no remote copies, remote signals or barrier semaphores. Data moves between devices by JAX's collectives and lax.ppermute only.
A program may use at most 128 MiB of HBM per device.

v0:
```python
import math
import jax
import jax.numpy as jnp
from jax import lax
from jax.sharding import PartitionSpec as P

HD = 128
BLOCK = 128
MAXPAGE = 8


def from_behind(block, axis, distance):
    devices = range(lax.axis_size(axis))
    route = [(i - distance, i) for i in devices if i - distance in devices]
    return lax.ppermute(block, axis, route)


def page_starts(page_ids):
    block_count = page_ids.shape[0]
    position = jnp.arange(block_count, dtype=jnp.int32)
    is_fresh = jnp.concatenate([jnp.ones((1,), dtype=jnp.bool_), page_ids[1:] != page_ids[:-1]])
    return lax.cummax(jnp.where(is_fresh, position, jnp.zeros_like(position)), axis=0)


def allowed_mask(global_block, padded_pages, starts, ref_row, block_size, window):
    nearby = lax.dynamic_slice_in_dim(padded_pages, global_block, window, 0)
    own_page = nearby[window - 1]
    inside = nearby == own_page
    offsets = jnp.arange(window)
    is_last = offsets == window - 1
    rows_at = jnp.arange(block_size)
    causal = rows_at[None, :] <= rows_at[:, None]
    window_ok = inside[None, :, None] & (
        jnp.logical_not(is_last)[None, :, None] | causal[:, None, :]
    )
    window_ok = window_ok.reshape(block_size, window * block_size)
    start_here = lax.dynamic_index_in_dim(starts, global_block, 0, keepdims=False)
    ref_ok = ref_row < start_here
    ref_ok = jnp.broadcast_to(ref_ok[None, :, None], (block_size, ref_row.shape[0], block_size))
    return jnp.concatenate([window_ok, ref_ok.reshape(block_size, -1)], axis=1)


def attend(query_block, key_set, value_set, allowed):
    score_scale = 1.0 / math.sqrt(query_block.shape[-1])
    scores = (
        jnp.einsum("tgqd,sgd->gqts", query_block, key_set, preferred_element_type=jnp.float32)
        * score_scale
    )
    scores = jnp.where(allowed, scores, -1e30)
    row_max = jnp.max(scores, axis=-1, keepdims=True)
    exp_scores = jnp.where(allowed, jnp.exp(scores - row_max), 0.0)
    totals = jnp.sum(exp_scores, axis=-1)
    weights = exp_scores.astype(jnp.bfloat16)
    mixture = jnp.einsum("gqts,sgd->tgqd", weights, value_set, preferred_element_type=jnp.float32)
    return (mixture / jnp.transpose(totals, (2, 0, 1))[..., None]).astype(jnp.bfloat16)


def shards(queries, key_states, value_states, page_ids, ref_group, ref_slot):
    head_queries, head_keys, head_values = (
        lax.all_to_all(queries, "head", split_axis=1, concat_axis=0, tiled=True),
        lax.all_to_all(key_states, "head", split_axis=1, concat_axis=0, tiled=True),
        lax.all_to_all(value_states, "head", split_axis=1, concat_axis=0, tiled=True),
    )
    group_tokens = head_keys.shape[0]
    key_width = head_keys.shape[1]
    local_heads = key_width // HD
    blocks = group_tokens // BLOCK
    reach = MAXPAGE - 1
    refs_count = ref_group.shape[1]
    key_blocks = head_keys.reshape(blocks, BLOCK, key_width)
    value_blocks = head_values.reshape(blocks, BLOCK, key_width)
    tail_keys, tail_values = from_behind(
        (key_blocks[blocks - reach :], value_blocks[blocks - reach :]), "ctx", 1
    )
    near_keys = jnp.concatenate([tail_keys, key_blocks])
    near_values = jnp.concatenate([tail_values, value_blocks])
    ctx_group = lax.axis_index("ctx")
    first_block = ctx_group * blocks
    own_groups = lax.dynamic_slice_in_dim(ref_group, first_block, blocks, 0)
    own_slots = lax.dynamic_slice_in_dim(ref_slot, first_block, blocks, 0)
    own_rows = own_groups * blocks + own_slots
    whole_keys, whole_values = (
        lax.all_gather(key_blocks, "ctx", axis=0, tiled=True),
        lax.all_gather(value_blocks, "ctx", axis=0, tiled=True),
    )
    flat_rows = own_rows.reshape(-1)
    far_keys = jnp.take(whole_keys, flat_rows, axis=0).reshape(blocks, refs_count, BLOCK, key_width)
    far_values = jnp.take(whole_values, flat_rows, axis=0).reshape(
        blocks, refs_count, BLOCK, key_width
    )
    padded_pages = jnp.concatenate([jnp.full((reach,), -1, dtype=jnp.int32), page_ids])
    starts = page_starts(page_ids)
    group_size = head_queries.shape[1] // key_width
    query_blocks = head_queries.reshape(blocks, BLOCK, local_heads, group_size, HD)

    def one_block(local_block):
        global_block = first_block + local_block
        ref_row = lax.dynamic_index_in_dim(own_rows, local_block, 0, keepdims=False)
        key_set = jnp.concatenate(
            [
                lax.dynamic_slice_in_dim(near_keys, local_block, MAXPAGE, 0),
                lax.dynamic_index_in_dim(far_keys, local_block, 0, keepdims=False),
            ]
        )
        value_set = jnp.concatenate(
            [
                lax.dynamic_slice_in_dim(near_values, local_block, MAXPAGE, 0),
                lax.dynamic_index_in_dim(far_values, local_block, 0, keepdims=False),
            ]
        )
        allowed = allowed_mask(global_block, padded_pages, starts, ref_row, BLOCK, MAXPAGE)
        query_block = lax.dynamic_index_in_dim(query_blocks, local_block, 0, keepdims=False)
        return attend(
            query_block,
            key_set.reshape(-1, local_heads, HD),
            value_set.reshape(-1, local_heads, HD),
            allowed,
        )

    outputs = lax.map(one_block, jnp.arange(blocks, dtype=jnp.int32))
    merged = outputs.reshape(group_tokens, head_queries.shape[1])
    return lax.all_to_all(merged, "head", split_axis=0, concat_axis=1, tiled=True)


def solution(mesh):
    placed = (
        P(("ctx", "head"), None),
        P(("ctx", "head"), None),
        P(("ctx", "head"), None),
        P(),
        P(),
        P(),
    )
    return jax.shard_map(
        shards, mesh=mesh, in_specs=placed, out_specs=P(("ctx", "head"), None), check_vma=False
    )
```

profile of v0, /device:TPU:1, one launch (start us, length us, event | category | flops | bytes accessed | tf_op | source)
XLA Modules:
  0.0 519.4 jit_solution(513064871498028624)
XLA Ops:
  7.7 15.0 %all_to_all.67 = bf16[256,8,128]{2,0,1:T(8,128)(2,1)} all-to-all(bf16[256,8,128]{2,0,1:T(8,128)(2,1)S(1)} %copy_bitcast_fusion.4), channel_id=1, replica_groups=mesh['ctx'=16,'head'=8] {'head'}, dimensions={1} | all-to-all | bytes 1048576 | tf_op jit(solution)/shard_map/all_to_all | solution.py:62
  23.9 13.4 %all_to_all.68 = bf16[256,8,128]{2,0,1:T(8,128)(2,1)} all-to-all(bf16[256,8,128]{2,0,1:T(8,128)(2,1)S(1)} %copy_bitcast_fusion.3), channel_id=1, replica_groups=mesh['ctx'=16,'head'=8] {'head'}, dimensions={1} | all-to-all | bytes 1048576 | tf_op jit(solution)/shard_map/all_to_all | solution.py:61
  37.4 4.8 copy.62
  42.2 5.6 %all-to-all-start.2 = ((bf16[256,8,1024]{2,0,1:T(8,128)(2,1)}), bf16[256,8,1024]{2,0,1:T(8,128)(2,1)}, u32[]{:S(2)}, u32[]{:S(2)}) async-start(bf16[256,8,1024]{2,0,1:T(8,128)(2,1)} %bitcast.164), calls=%async_computation.2 | async-start | bytes 8388608 | tf_op jit(solution)/shard_map/all_to_all | solution.py:60
  49.0 3.2 collective-permute-start
  52.3 3.2 collective-permute-start.1
  58.0 8.6 %collective-permute-done.1 = bf16[7,128,128]{2,1,0:T(8,128)(2,1)S(1)} collective-permute-done((bf16[7,128,128]{2,1,0:T(8,128)(2,1)S(1)}, bf16[7,128,128]{2,1,0:T(8,128)(2,1)S(1)}, u32[]{:S(2)}, u32[]{:S(2)}) %collective-permute-start.1) | collective-permute-done | bytes 229408 | tf_op jit(solution)/shard_map/ppermute | solution.py:15
  67.5 29.1 %all-to-all-done.2 = bf16[256,8,1024]{2,0,1:T(8,128)(2,1)} async-done(((bf16[256,8,1024]{2,0,1:T(8,128)(2,1)}), bf16[256,8,1024]{2,0,1:T(8,128)(2,1)}, u32[]{:S(2)}, u32[]{:S(2)}) %all-to-all-start.2) | async-done | bytes 4194336 | tf_op jit(solution)/shard_map/all_to_all | solution.py:60
  96.6 5.2 %copy.54 = bf16[256,8,8,128]{3,2,1,0:T(8,128)(2,1)} copy(bf16[256,8,8,128]{3,1,2,0:T(8,128)(2,1)} %bitcast.50) | data formatting | bytes 8388608
  101.8 4.3 gather_fusion
  106.1 66.7 %all-gather.5.cloned.1.call-done = bf16[256,128,128]{2,1,0:T(8,128)(2,1)} async-done(((bf16[16,128,128]{2,1,0:T(8,128)(2,1)}), bf16[256,128,128]{2,1,0:T(8,128)(2,1)}) %all-gather.5.cloned.1.call-update) | async-done | bytes 8388624 | tf_op jit(solution)/shard_map/all_gather | solution.py:83
  172.9 5.6 %gather_fusion.1 = bf16[64,128,128]{2,1,0:T(8,128)(2,1)} fusion(bf16[256,128,128]{2,1,0:T(8,128)(2,1)} %all-gather.5.cloned.1.call-done, s32[1024]{0:T(1024)S(1)} %pad_clamp_fusion), kind=kCustom, calls=%fused_computation.1.clone | custom fusion | bytes 4194560 | tf_op jit(solution)/shard_map/jit(_take)/gather | solution.py:87
  178.4 4.0 broadcast_select_fusion
  182.4 256.0 %while.10 = (s32[]{:T(128)}, bf16[16,128,1,8,128]{4,3,1,0,2:T(8,128)(2,1)}, s32[16]{0:T(128)S(1)}, bf16[23,128,128]{2,1,0:T(8,128)(2,1)}, bf16[16,4,128,128]{3,2...) while((s32[]{:T(128)}, ...), condition=%wide.region_5.7_spmd, body=%wide.region_2.6_spmd.sunk | while | flops 826882048 | bytes 26014728 | solution.py:120
  195.8 1.7 fusion.42
  227.8 1.7 fusion.42
  243.8 1.7 fusion.42
  259.8 1.7 fusion.42
  275.8 1.7 fusion.42
  291.8 1.7 fusion.42
  438.4 7.3 %all_to_all.59 = bf16[8,256,1024]{2,1,0:T(8,128)(2,1)} reshape(bf16[16,128,1,8,128]{4,3,1,0,2:T(8,128)(2,1)} %get-tuple-element.68) | data formatting | bytes 8388608 | tf_op jit(solution)/shard_map/all_to_all | solution.py:122
  445.8 54.0 %all_to_all.69 = bf16[8,256,1024]{2,1,0:T(8,128)(2,1)} all-to-all(bf16[8,256,1024]{2,1,0:T(8,128)(2,1)} %all_to_all.59), channel_id=1, replica_groups=mesh['ctx'=16,'head'=8] {'head'}, dimensions={0} | all-to-all | bytes 8388608 | tf_op jit(solution)/shard_map/all_to_all | solution.py:122
  499.7 6.5 %copy.41 = bf16[256,8,1024]{0,2,1:T(8,128)(2,1)} copy(bf16[256,8,1024]{2,0,1:T(8,128)(2,1)} %bitcast.165) | data formatting | bytes 8388608 | tf_op jit(solution)/shard_map/all_to_all | solution.py:122
  506.2 6.4 %copy.42 = bf16[256,8192]{1,0:T(8,128)(2,1)} copy(bf16[256,8192]{0,1:T(8,128)(2,1)} %bitcast.166) | data formatting | bytes 8388608 | tf_op jit(solution)/shard_map/all_to_all | solution.py:122
  (406 shorter events, 190.6 us)
Async XLA Ops:
  6.5 1.0 copy-start
  6.5 95.3 %all-gather.3.cloned.1.call-start = ((), (), s32[]{:S(2)}) async-start(), calls=%async_computation.4 | async-start | bytes 8912896 | tf_op jit(solution)/shard_map/all_gather | solution.py:84
  22.7 150.2 %all-gather.5.cloned.1.call-start = ((), (), s32[]{:S(2)}) async-start(), calls=%async_computation.5 | async-start | bytes 8912896 | tf_op jit(solution)/shard_map/all_gather | solution.py:83
  42.1 5.6 %copy-start.5 = (s32[256,4]{0,1:T(4,128)S(1)}, s32[256,4]{0,1:T(4,128)}, u32[]{:S(2)}) copy-start(s32[256,4]{0,1:T(4,128)} %param.15) | copy-start | bytes 12292
  42.1 5.6 %copy-start.6 = (s32[256,4]{0,1:T(4,128)S(1)}, s32[256,4]{0,1:T(4,128)}, u32[]{:S(2)}) copy-start(s32[256,4]{0,1:T(4,128)} %param.14) | copy-start | bytes 12292
  42.2 6.0 %copy-start.4 = (s32[256]{0:T(256)S(1)}, s32[256]{0:T(256)}, u32[]{:S(2)}) copy-start(s32[256]{0:T(256)} %param.13) | copy-start | bytes 3076
  42.2 6.8 %copy-start.2 = (bf16[256,8,128]{2,0,1:T(8,128)(2,1)S(1)}, bf16[256,8,128]{2,0,1:T(8,128)(2,1)}, u32[]{:S(2)}) copy-start(bf16[256,8,128]{2,0,1:T(8,128)(2,1)} %all_to_all.67) | copy-start | bytes 1572868
  42.2 10.1 %copy-start.3 = (bf16[256,8,128]{2,0,1:T(8,128)(2,1)S(1)}, bf16[256,8,128]{2,0,1:T(8,128)(2,1)}, u32[]{:S(2)}) copy-start(bf16[256,8,128]{2,0,1:T(8,128)(2,1)} %all_to_all.68) | copy-start | bytes 1572868
  42.2 54.4 %all-to-all-start.2 = ((bf16[256,8,1024]{2,0,1:T(8,128)(2,1)}), bf16[256,8,1024]{2,0,1:T(8,128)(2,1)}, u32[]{:S(2)}, u32[]{:S(2)}) async-start(bf16[256,8,1024]{2,0,1:T(8,128)(2,1)} %bitcast.164), calls=%async_computation.2 | async-start | bytes 8388608 | tf_op jit(solution)/shard_map/all_to_all | solution.py:60
  49.0 8.0 %collective-permute-start = (bf16[7,128,128]{2,1,0:T(8,128)(2,1)S(1)}, bf16[7,128,128]{2,1,0:T(8,128)(2,1)S(1)}, u32[]{:S(2)}, u32[]{:S(2)}) collective-permute-start(bf16[7,128,128]{2,1,0:T(8,128)(2,1)S(1)} %slice.32), channel_id=1, source_target_pairs={{0,8},{8,16},{16,24},{24,32},{32,40},{40,48},{48,56},{56,64},{64,7... | collective-permute-start | bytes 688136 | tf_op jit(solution)/shard_map/ppermute | solution.py:15
  52.3 14.3 %collective-permute-start.1 = (bf16[7,128,128]{2,1,0:T(8,128)(2,1)S(1)}, bf16[7,128,128]{2,1,0:T(8,128)(2,1)S(1)}, u32[]{:S(2)}, u32[]{:S(2)}) collective-permute-start(bf16[7,128,128]{2,1,0:T(8,128)(2,1)S(1)} %slice.33), channel_id=1, source_target_pairs={{0,8},{8,16},{16,24},{24,32},{32,40},{40,48},{48,56},{56,64},{64,7... | collective-permute-start | bytes 688136 | tf_op jit(solution)/shard_map/ppermute | solution.py:15
  506.2 6.4 %copy-start.1 = (bf16[256,1024]{1,0:T(8,128)(2,1)S(1)}, bf16[256,1024]{1,0:T(8,128)(2,1)}, u32[]{:S(2)}) copy-start(bf16[256,1024]{1,0:T(8,128)(2,1)} %param.12) | copy-start | bytes 1572868
Sparse Core Ops, SparseCore 0:
  22.8 77.1 all-gather.2
  102.2 70.6 all-gather.4
where the time goes:
time: 523 us; the launch traced here: 519 us
  local copies, waits for them, and re-layouts  139 us (27%)
  waiting for transfers between devices  106 us (20%)
  blocking collectives  82.4 us (16%)
  loops' own time  62.4 us (12%)
  other arithmetic  61.2 us (12%)
  matrix products  43.3 us (8%)
  between operations  13.5 us (3%)
  starting transfers between devices  12.1 us (2%)
    all_gather x1, waiting for transfers between devices, shards(): lax.all_gather(key_blocks, 'ctx', axis=0, tiled=True)  66.7 us
    another operation x1, loops' own time, shards(): outputs = lax.map(one_block, jnp.arange(blocks, dtype=jnp.int32))  62.4 us
    all_to_all x1, blocking collectives, shards(): lax.all_to_all(merged, 'head', split_axis=0, concat_axis=1, tiled=True)  54 us
    all_to_all x1, waiting for transfers between devices, shards(): lax.all_to_all(queries, 'head', split_axis=1, concat_axis=0, tiled=True)  29.1 us
    dot_general x16, matrix products, attend(): jnp.einsum('gqts,sgd->tgqd', weights, value_set, preferred_element_type=j...  26.6 us
    reduce_sum x16, other arithmetic, attend(): totals = jnp.sum(exp_scores, axis=-1)  24.1 us
    all_to_all x3, local copies, waits for them, and re-layouts, shards(): lax.all_to_all(merged, 'head', split_axis=0, concat_axis=1, tiled=True)  20.2 us
    dynamic_slice x16, local copies, waits for them, and re-layouts, one_block(): lax.dynamic_slice_in_dim(near_keys, local_block, MAXPAGE, 0)  17.1 us
  transfers between devices with their start and end apart: 5, of which 4 were waited for; matrix products, arithmetic and copies ran while one was open for 4% of the time, Pallas kernels for 0%

commit v1 on v0

--- a/solution.py
+++ b/solution.py
@@ -7,6 +7,24 @@
 HD = 128
 BLOCK = 128
 MAXPAGE = 8
+
+
+def gather_around(array, axis, dim):
+    ways, here, hop = (lax.axis_size(axis), lax.axis_index(axis), array.shape[dim])
+    dims = [n * ways if d == dim else n for d, n in enumerate(array.shape)]
+    full = lax.dynamic_update_slice_in_dim(
+        jnp.zeros(dims, array.dtype), array, here * hop, axis=dim
+    )
+    going_up = going_down = array
+    for far in range(1, ways // 2 + 1):
+        going_up = lax.ppermute(going_up, axis, [(d, (d + 1) % ways) for d in range(ways)])
+        full = lax.dynamic_update_slice_in_dim(full, going_up, (here - far) % ways * hop, axis=dim)
+        if 2 * far < ways:
+            going_down = lax.ppermute(going_down, axis, [(d, (d - 1) % ways) for d in range(ways)])
+            full = lax.dynamic_update_slice_in_dim(
+                full, going_down, (here + far) % ways * hop, axis=dim
+            )
+    return full
 
 
 def from_behind(block, axis, distance):
@@ -80,7 +98,7 @@
     own_slots = lax.dynamic_slice_in_dim(ref_slot, first_block, blocks, 0)
     own_rows = own_groups * blocks + own_slots
     whole_keys, whole_values = (
-        lax.all_gather(key_blocks, "ctx", axis=0, tiled=True),
+        gather_around(key_blocks, "ctx", 0),
         lax.all_gather(value_blocks, "ctx", axis=0, tiled=True),
     )
     flat_rows = own_rows.reshape(-1)

time: 523 us -> 554 us (1.059)
  starting transfers between devices: 12.1 us -> 46.7 us
  waiting for transfers between devices: 106 us -> 71.7 us
  local copies, waits for them, and re-layouts: 139 us -> 163 us
    ppermute x0 -> x15, waiting for transfers between devices: none -> 68.2 us  [the longest x7 35.4 us: gather_around(): lax.ppermute(going_down, axis, [(d, (d - 1) % ways) for d in range(ways)])]
    all_gather x1 -> x0, waiting for transfers between devices: 66.7 us -> none  [shards(): lax.all_gather(key_blocks, 'ctx', axis=0, tiled=True)]
    ppermute x0 -> x15, starting transfers between devices: none -> 38.5 us  [the longest x7 33 us: gather_around(): lax.ppermute(going_down, axis, [(d, (d - 1) % ways) for d in range(ways)])]
    all_to_all x1, waiting for transfers between devices: 29.1 us -> 0.01 us  [shards(): lax.all_to_all(queries, 'head', split_axis=1, concat_axis=0, tiled=True)]
    dynamic_update_slice x0 -> x16, local copies, waits for them, and re-layouts: none -> 17.8 us  [the longest x8 8.85 us: gather_around(): lax.dynamic_update_slice_in_dim(full, going_up, (here - far) % ways * hop...]
    ppermute x2, waiting for transfers between devices: 10 us -> 3.48 us  [from_behind(): return lax.ppermute(block, axis, route)]
  transfers between devices with their start and end apart: 5 -> 19, of which waited for: 4 -> 12; matrix products, arithmetic and copies ran while one was open for 4% -> 7% of each run, Pallas kernels for 0% -> 0%
where the time goes in v1:
time: 554 us; the launch traced here: 551 us
  local copies, waits for them, and re-layouts  163 us (29%)
  blocking collectives  85.4 us (15%)
  waiting for transfers between devices  71.7 us (13%)
  other arithmetic  64.7 us (12%)
  loops' own time  62.2 us (11%)
  starting transfers between devices  46.7 us (8%)
  matrix products  43.4 us (8%)
  between operations  13.5 us (2%)
    another operation x1, loops' own time, shards(): outputs = lax.map(one_block, jnp.arange(blocks, dtype=jnp.int32))  62.2 us
    all_to_all x1, blocking collectives, shards(): lax.all_to_all(merged, 'head', split_axis=0, concat_axis=1, tiled=True)  57.6 us
    ppermute x7, waiting for transfers between devices, gather_around(): lax.ppermute(going_down, axis, [(d, (d - 1) % ways) for d in range(ways)])  35.4 us
    ppermute x7, starting transfers between devices, gather_around(): lax.ppermute(going_down, axis, [(d, (d - 1) % ways) for d in range(ways)])  33 us
    ppermute x8, waiting for transfers between devices, gather_around(): lax.ppermute(going_up, axis, [(d, (d + 1) % ways) for d in range(ways)])  32.8 us
    dot_general x16, matrix products, attend(): jnp.einsum('gqts,sgd->tgqd', weights, value_set, preferred_element_type=j...  26.7 us
    reduce_sum x16, other arithmetic, attend(): totals = jnp.sum(exp_scores, axis=-1)  24.3 us
    all_to_all x3, local copies, waits for them, and re-layouts, shards(): lax.all_to_all(merged, 'head', split_axis=0, concat_axis=1, tiled=True)  20.2 us
  transfers between devices with their start and end apart: 19, of which 12 were waited for; matrix products, arithmetic and copies ran while one was open for 7% of the time, Pallas kernels for 0%

profile of v1, /device:TPU:1, one launch (start us, length us, event | category | flops | bytes accessed | tf_op | source)
XLA Modules:
  0.0 550.8 jit_solution(9582360999959723014)
XLA Ops:
  7.7 15.0 %all_to_all.67 = bf16[256,8,128]{2,0,1:T(8,128)(2,1)} all-to-all(bf16[256,8,128]{2,0,1:T(8,128)(2,1)S(1)} %copy_bitcast_fusion.4), channel_id=1, replica_groups=mesh['ctx'=16,'head'=8] {'head'}, dimensions={1} | all-to-all | bytes 1048576 | tf_op jit(solution)/shard_map/all_to_all | solution.py:80
  23.9 12.8 %all_to_all.68 = bf16[256,8,128]{2,0,1:T(8,128)(2,1)S(1)} all-to-all(bf16[256,8,128]{2,0,1:T(8,128)(2,1)S(1)} %copy_bitcast_fusion.3), channel_id=1, replica_groups=mesh['ctx'=16,'head'=8] {'head'}, dimensions={1} | all-to-all | bytes 1048576 | tf_op jit(solution)/shard_map/all_to_all | solution.py:79
  37.9 5.0 collective-permute-start.3
  42.9 17.0 %collective-permute-done.2 = bf16[16,128,128]{2,1,0:T(8,128)(2,1)S(1)} collective-permute-done((bf16[16,128,128]{2,1,0:T(8,128)(2,1)S(1)}, bf16[16,128,128]{2,1,0:T(8,128)(2,1)S(1)}, u32[]{:S(2)}, u32[]{:S(2)}) %collective-permute-start.2) | collective-permute-done | bytes 524320 | tf_op jit(solution)/shard_map/ppermute | solution.py:20
  59.9 4.8 copy.62
  64.7 5.5 %all-to-all-start.2 = ((bf16[256,8,1024]{2,0,1:T(8,128)(2,1)}), bf16[256,8,1024]{2,0,1:T(8,128)(2,1)}, u32[]{:S(2)}, u32[]{:S(2)}) async-start(bf16[256,8,1024]{2,0,1:T(8,128)(2,1)} %bitcast.164), calls=%async_computation.2 | async-start | bytes 8388608 | tf_op jit(solution)/shard_map/all_to_all | solution.py:78
  70.2 5.1 collective-permute-start.5
  79.3 18.9 %collective-permute-done.5 = bf16[16,128,128]{2,1,0:T(8,128)(2,1)S(1)} collective-permute-done((bf16[16,128,128]{2,1,0:T(8,128)(2,1)S(1)}, bf16[16,128,128]{2,1,0:T(8,128)(2,1)S(1)}, u32[]{:S(2)}, u32[]{:S(2)}) %collective-permute-start.5) | collective-permute-done | bytes 524320 | tf_op jit(solution)/shard_map/ppermute | solution.py:23
  98.2 5.5 %collective-permute-start.7 = (bf16[16,128,128]{2,1,0:T(8,128)(2,1)S(1)}, bf16[16,128,128]{2,1,0:T(8,128)(2,1)}, u32[]{:S(2)}, u32[]{:S(2)}) collective-permute-start(bf16[16,128,128]{2,1,0:T(8,128)(2,1)S(1)} %collective-permute-done.5), channel_id=1, source_target_pairs={{0,120},{8,0},{16,8},{24,16},{32,24},{40,32},{48,40},{56,48},{64,5... | collective-permute-start | bytes 1572872 | tf_op jit(solution)/shard_map/ppermute | solution.py:23
  106.7 16.5 %collective-permute-done.7 = bf16[16,128,128]{2,1,0:T(8,128)(2,1)} collective-permute-done((bf16[16,128,128]{2,1,0:T(8,128)(2,1)S(1)}, bf16[16,128,128]{2,1,0:T(8,128)(2,1)}, u32[]{:S(2)}, u32[]{:S(2)}) %collective-permute-start.7) | collective-permute-done | bytes 524320 | tf_op jit(solution)/shard_map/ppermute | solution.py:23
  123.2 4.9 collective-permute-start.9
  134.4 5.3 broadcast_in_dim.53
  140.7 4.7 collective-permute-start.11
  154.7 5.3 collective-permute-start.13
  179.0 5.3 copy.54
  186.0 3.7 collective-permute-done.16
  190.7 4.3 gather_fusion.1
  195.0 5.6 %gather_fusion = bf16[64,128,128]{2,1,0:T(8,128)(2,1)} fusion(bf16[256,128,128]{2,1,0:T(8,128)(2,1)} %all-gather.2.cloned.1.call-done, s32[1024]{0:T(1024)S(1)} %pad_clamp_fusion), kind=kCustom, calls=%fused_computation.clone | custom fusion | bytes 4194560 | tf_op jit(solution)/shard_map/jit(_take)/gather | solution.py:106
  200.6 4.0 broadcast_select_fusion
  204.6 261.5 %while.10 = (s32[]{:T(128)}, bf16[16,128,1,8,128]{4,3,1,0,2:T(8,128)(2,1)}, s32[16]{0:T(128)S(1)}, bf16[23,128,128]{2,1,0:T(8,128)(2,1)}, bf16[16,4,128,128]{3,2...) while((s32[]{:T(128)}, ...), condition=%wide.region_5.7_spmd, body=%wide.region_2.6_spmd.sunk | while | flops 826882048 | bytes 26014728 | solution.py:138
  466.1 7.3 %all_to_all.59 = bf16[8,256,1024]{2,1,0:T(8,128)(2,1)} reshape(bf16[16,128,1,8,128]{4,3,1,0,2:T(8,128)(2,1)} %get-tuple-element.68) | data formatting | bytes 8388608 | tf_op jit(solution)/shard_map/all_to_all | solution.py:140
  473.4 57.6 %all_to_all.69 = bf16[8,256,1024]{2,1,0:T(8,128)(2,1)} all-to-all(bf16[8,256,1024]{2,1,0:T(8,128)(2,1)} %all_to_all.59), channel_id=1, replica_groups=mesh['ctx'=16,'head'=8] {'head'}, dimensions={0} | all-to-all | bytes 8388608 | tf_op jit(solution)/shard_map/all_to_all | solution.py:140
  531.1 6.6 %copy.41 = bf16[256,8,1024]{0,2,1:T(8,128)(2,1)} copy(bf16[256,8,1024]{2,0,1:T(8,128)(2,1)} %bitcast.165) | data formatting | bytes 8388608 | tf_op jit(solution)/shard_map/all_to_all | solution.py:140
  537.6 6.3 %copy.42 = bf16[256,8192]{1,0:T(8,128)(2,1)} copy(bf16[256,8192]{0,1:T(8,128)(2,1)} %bitcast.166) | data formatting | bytes 8388608 | tf_op jit(solution)/shard_map/all_to_all | solution.py:140
  (452 shorter events, 248.0 us)
Async XLA Ops:
  6.5 188.5 %all-gather.2.cloned.1.call-start = ((), (), s32[]{:S(2)}) async-start(), calls=%async_computation.4 | async-start | bytes 8912896 | tf_op jit(solution)/shard_map/all_gather | solution.py:102
  36.6 23.3 %collective-permute-start.2 = (bf16[16,128,128]{2,1,0:T(8,128)(2,1)S(1)}, bf16[16,128,128]{2,1,0:T(8,128)(2,1)S(1)}, u32[]{:S(2)}, u32[]{:S(2)}) collective-permute-start(bf16[16,128,128]{2,1,0:T(8,128)(2,1)S(1)} %bitcast.172), channel_id=1, source_target_pairs={{0,8},{8,16},{16,24},{24,32},{32,40},{40,48},{48,56},{56,64},{64,7... | collective-permute-start | bytes 1572872 | tf_op jit(solution)/shard_map/ppermute | solution.py:20
  37.9 32.3 %collective-permute-start.3 = (bf16[16,128,128]{2,1,0:T(8,128)(2,1)S(1)}, bf16[16,128,128]{2,1,0:T(8,128)(2,1)S(1)}, u32[]{:S(2)}, u32[]{:S(2)}) collective-permute-start(bf16[16,128,128]{2,1,0:T(8,128)(2,1)S(1)} %bitcast.173), channel_id=1, source_target_pairs={{0,120},{8,0},{16,8},{24,16},{32,24},{40,32},{48,40},{56,48},{64,5... | collective-permute-start | bytes 1572872 | tf_op jit(solution)/shard_map/ppermute | solution.py:23
  59.9 19.4 %collective-permute-start.4 = (bf16[16,128,128]{2,1,0:T(8,128)(2,1)S(1)}, bf16[16,128,128]{2,1,0:T(8,128)(2,1)S(1)}, u32[]{:S(2)}, u32[]{:S(2)}) collective-permute-start(bf16[16,128,128]{2,1,0:T(8,128)(2,1)S(1)} %collective-permute-done.2), channel_id=1, source_target_pairs={{0,8},{8,16},{16,24},{24,32},{32,40},{40,48},{48,56},{56,64},{64,7... | collective-permute-start | bytes 1572872 | tf_op jit(solution)/shard_map/ppermute | solution.py:20
  64.7 39.0 %copy-start.5 = (s32[256]{0:T(256)S(1)}, s32[256]{0:T(256)}, u32[]{:S(2)}) copy-start(s32[256]{0:T(256)} %param.13) | copy-start | bytes 3076
  64.7 68.4 %copy-start.2 = (bf16[256,8,128]{2,0,1:T(8,128)(2,1)S(1)}, bf16[256,8,128]{2,0,1:T(8,128)(2,1)}, u32[]{:S(2)}) copy-start(bf16[256,8,128]{2,0,1:T(8,128)(2,1)} %all_to_all.67) | copy-start | bytes 1572868
  64.7 114.3 %all-to-all-start.2 = ((bf16[256,8,1024]{2,0,1:T(8,128)(2,1)}), bf16[256,8,1024]{2,0,1:T(8,128)(2,1)}, u32[]{:S(2)}, u32[]{:S(2)}) async-start(bf16[256,8,1024]{2,0,1:T(8,128)(2,1)} %bitcast.164), calls=%async_computation.2 | async-start | bytes 8388608 | tf_op jit(solution)/shard_map/all_to_all | solution.py:78
  70.2 27.9 %collective-permute-start.5 = (bf16[16,128,128]{2,1,0:T(8,128)(2,1)S(1)}, bf16[16,128,128]{2,1,0:T(8,128)(2,1)S(1)}, u32[]{:S(2)}, u32[]{:S(2)}) collective-permute-start(bf16[16,128,128]{2,1,0:T(8,128)(2,1)S(1)} %collective-permute-done.3), channel_id=1, source_target_pairs={{0,120},{8,0},{16,8},{24,16},{32,24},{40,32},{48,40},{56,48},{64,5... | collective-permute-start | bytes 1572872 | tf_op jit(solution)/shard_map/ppermute | solution.py:23
  79.3 27.2 %collective-permute-start.6 = (bf16[16,128,128]{2,1,0:T(8,128)(2,1)S(1)}, bf16[16,128,128]{2,1,0:T(8,128)(2,1)}, u32[]{:S(2)}, u32[]{:S(2)}) collective-permute-start(bf16[16,128,128]{2,1,0:T(8,128)(2,1)S(1)} %collective-permute-done.4), channel_id=1, source_target_pairs={{0,8},{8,16},{16,24},{24,32},{32,40},{40,48},{48,56},{56,64},{64,7... | collective-permute-start | bytes 1572872 | tf_op jit(solution)/shard_map/ppermute | solution.py:20
  98.2 47.2 %copy-start.3 = (bf16[16,128,128]{2,1,0:T(8,128)(2,1)}, bf16[16,128,128]{2,1,0:T(8,128)(2,1)S(1)}, u32[]{:S(2)}) copy-start(bf16[16,128,128]{2,1,0:T(8,128)(2,1)S(1)} %collective-permute-done.5) | copy-start | bytes 1572868
  98.2 25.0 %collective-permute-start.7 = (bf16[16,128,128]{2,1,0:T(8,128)(2,1)S(1)}, bf16[16,128,128]{2,1,0:T(8,128)(2,1)}, u32[]{:S(2)}, u32[]{:S(2)}) collective-permute-start(bf16[16,128,128]{2,1,0:T(8,128)(2,1)S(1)} %collective-permute-done.5), channel_id=1, source_target_pairs={{0,120},{8,0},{16,8},{24,16},{32,24},{40,32},{48,40},{56,48},{64,5... | collective-permute-start | bytes 1572872 | tf_op jit(solution)/shard_map/ppermute | solution.py:23
  106.5 25.2 %collective-permute-start.8 = (bf16[16,128,128]{2,1,0:T(8,128)(2,1)}, bf16[16,128,128]{2,1,0:T(8,128)(2,1)}, u32[]{:S(2)}, u32[]{:S(2)}) collective-permute-start(bf16[16,128,128]{2,1,0:T(8,128)(2,1)} %collective-permute-done.6), channel_id=1, source_target_pairs={{0,8},{8,16},{16,24},{24,32},{32,40},{40,48},{48,56},{56,64},{64,7... | collective-permute-start | bytes 1572872 | tf_op jit(solution)/shard_map/ppermute | solution.py:20
  123.2 17.5 %collective-permute-start.9 = (bf16[16,128,128]{2,1,0:T(8,128)(2,1)}, bf16[16,128,128]{2,1,0:T(8,128)(2,1)}, u32[]{:S(2)}, u32[]{:S(2)}) collective-permute-start(bf16[16,128,128]{2,1,0:T(8,128)(2,1)} %collective-permute-done.7), channel_id=1, source_target_pairs={{0,120},{8,0},{16,8},{24,16},{32,24},{40,32},{48,40},{56,48},{64,5... | collective-permute-start | bytes 1572872 | tf_op jit(solution)/shard_map/ppermute | solution.py:23
  131.7 14.9 %collective-permute-start.10 = (bf16[16,128,128]{2,1,0:T(8,128)(2,1)}, bf16[16,128,128]{2,1,0:T(8,128)(2,1)S(1)}, u32[]{:S(2)}, u32[]{:S(2)}) collective-permute-start(bf16[16,128,128]{2,1,0:T(8,128)(2,1)} %collective-permute-done.8), channel_id=1, source_target_pairs={{0,8},{8,16},{16,24},{24,32},{32,40},{40,48},{48,56},{56,64},{64,7... | collective-permute-start | bytes 1572872 | tf_op jit(solution)/shard_map/ppermute | solution.py:20
  131.7 14.5 %collective-permute-start.1 = (bf16[7,128,128]{2,1,0:T(8,128)(2,1)S(1)}, bf16[7,128,128]{2,1,0:T(8,128)(2,1)S(1)}, u32[]{:S(2)}, u32[]{:S(2)}) collective-permute-start(bf16[7,128,128]{2,1,0:T(8,128)(2,1)S(1)} %slice.33), channel_id=1, source_target_pairs={{0,8},{8,16},{16,24},{24,32},{32,40},{40,48},{48,56},{56,64},{64,7... | collective-permute-start | bytes 688136 | tf_op jit(solution)/shard_map/ppermute | solution.py:33
  133.1 18.1 %collective-permute-start = (bf16[7,128,128]{2,1,0:T(8,128)(2,1)S(1)}, bf16[7,128,128]{2,1,0:T(8,128)(2,1)S(1)}, u32[]{:S(2)}, u32[]{:S(2)}) collective-permute-start(bf16[7,128,128]{2,1,0:T(8,128)(2,1)S(1)} %slice.32), channel_id=1, source_target_pairs={{0,8},{8,16},{16,24},{24,32},{32,40},{40,48},{48,56},{56,64},{64,7... | collective-permute-start | bytes 688136 | tf_op jit(solution)/shard_map/ppermute | solution.py:33
  140.7 14.0 %collective-permute-start.11 = (bf16[16,128,128]{2,1,0:T(8,128)(2,1)}, bf16[16,128,128]{2,1,0:T(8,128)(2,1)S(1)}, u32[]{:S(2)}, u32[]{:S(2)}) collective-permute-start(bf16[16,128,128]{2,1,0:T(8,128)(2,1)} %collective-permute-done.9), channel_id=1, source_target_pairs={{0,120},{8,0},{16,8},{24,16},{32,24},{40,32},{48,40},{56,48},{64,5... | collective-permute-start | bytes 1572872 | tf_op jit(solution)/shard_map/ppermute | solution.py:23
  146.3 13.7 %copy-start.4 = (bf16[16,128,128]{2,1,0:T(8,128)(2,1)S(1)}, bf16[16,128,128]{2,1,0:T(8,128)(2,1)}, u32[]{:S(2)}) copy-start(bf16[16,128,128]{2,1,0:T(8,128)(2,1)} %copy-done.3) | copy-start | bytes 1572868
  146.6 15.8 %collective-permute-start.12 = (bf16[16,128,128]{2,1,0:T(8,128)(2,1)S(1)}, bf16[16,128,128]{2,1,0:T(8,128)(2,1)S(1)}, u32[]{:S(2)}, u32[]{:S(2)}) collective-permute-start(bf16[16,128,128]{2,1,0:T(8,128)(2,1)S(1)} %collective-permute-done.10), channel_id=1, source_target_pairs={{0,8},{8,16},{16,24},{24,32},{32,40},{40,48},{48,56},{56,64},{64,7... | collective-permute-start | bytes 1572872 | tf_op jit(solution)/shard_map/ppermute | solution.py:20
  154.7 17.5 %collective-permute-start.13 = (bf16[16,128,128]{2,1,0:T(8,128)(2,1)S(1)}, bf16[16,128,128]{2,1,0:T(8,128)(2,1)S(1)}, u32[]{:S(2)}, u32[]{:S(2)}) collective-permute-start(bf16[16,128,128]{2,1,0:T(8,128)(2,1)S(1)} %collective-permute-done.11), channel_id=1, source_target_pairs={{0,120},{8,0},{16,8},{24,16},{32,24},{40,32},{48,40},{56,48},{64,5... | collective-permute-start | bytes 1572872 | tf_op jit(solution)/shard_map/ppermute | solution.py:23
  162.4 14.1 %collective-permute-start.14 = (bf16[16,128,128]{2,1,0:T(8,128)(2,1)S(1)}, bf16[16,128,128]{2,1,0:T(8,128)(2,1)S(1)}, u32[]{:S(2)}, u32[]{:S(2)}) collective-permute-start(bf16[16,128,128]{2,1,0:T(8,128)(2,1)S(1)} %collective-permute-done.12), channel_id=1, source_target_pairs={{0,8},{8,16},{16,24},{24,32},{32,40},{40,48},{48,56},{56,64},{64,7... | collective-permute-start | bytes 1572872 | tf_op jit(solution)/shard_map/ppermute | solution.py:20
  172.2 12.9 %collective-permute-start.15 = (bf16[16,128,128]{2,1,0:T(8,128)(2,1)S(1)}, bf16[16,128,128]{2,1,0:T(8,128)(2,1)S(1)}, u32[]{:S(2)}, u32[]{:S(2)}) collective-permute-start(bf16[16,128,128]{2,1,0:T(8,128)(2,1)S(1)} %collective-permute-done.13), channel_id=1, source_target_pairs={{0,120},{8,0},{16,8},{24,16},{32,24},{40,32},{48,40},{56,48},{64,5... | collective-permute-start | bytes 1572872 | tf_op jit(solution)/shard_map/ppermute | solution.py:23
  176.5 13.2 %collective-permute-start.16 = (bf16[16,128,128]{2,1,0:T(8,128)(2,1)S(1)}, bf16[16,128,128]{2,1,0:T(8,128)(2,1)S(1)}, u32[]{:S(2)}, u32[]{:S(2)}) collective-permute-start(bf16[16,128,128]{2,1,0:T(8,128)(2,1)S(1)} %collective-permute-done.14), channel_id=1, source_target_pairs={{0,8},{8,16},{16,24},{24,32},{32,40},{40,48},{48,56},{56,64},{64,7... | collective-permute-start | bytes 1572872 | tf_op jit(solution)/shard_map/ppermute | solution.py:20
  531.1 12.9 %copy-start.1 = (bf16[256,1024]{1,0:T(8,128)(2,1)S(1)}, bf16[256,1024]{1,0:T(8,128)(2,1)}, u32[]{:S(2)}) copy-start(bf16[256,1024]{1,0:T(8,128)(2,1)} %param.12) | copy-start | bytes 1572868
  (3 other events, 22.2 us)
Sparse Core Ops, SparseCore 0:
  22.8 107.1 all-gather.1
